TPU v7x, 128 devices: a whole 4x4x4 slice. The times are simulated.
128 devices in a mesh: req: 32 (over x, z, core), tp: 4 (over y).
Axes of the slice: x: 4, y: 4, z: 4, core: 2. Of those that a mesh axis runs over, the one named last changes fastest.
Arguments:
- hidden: bfloat16 [8192, 2048], P('req', 'tp'), may hold values from -45 to 45
- routes: int32 [8192, 2], P('req'), may hold values from 0 to 7, all different within a row; in each aligned block of 256 rows (0 to 255, 256 to 511, ...) at most 128 rows name the same one
- route_weights: float32 [8192, 2], P('req'), may hold values from 0.2 to 1
- pre_gain: float32 [2048], replicated, may hold values from 0.1 to 1.9
- out_gain: float32 [2048], P('tp'), may hold values from 0.1 to 1.9
- gate_weight: bfloat16 [32, 2048, 5632], P('req', None, 'tp'), as said below
- up_weight: bfloat16 [32, 2048, 5632], P('req', None, 'tp'), as said below
- down_weight: bfloat16 [32, 5632, 2048], P('req', 'tp'), as said below
Outputs:
- residual_out: bfloat16 [8192, 2048], P('req', 'tp')
- normed_out: bfloat16 [8192, 2048], P('req', 'tp')
Inputs may be any that keep to these rules, and one draw needn't show every extreme that they name: `routes`: each row names 2 different experts; in the rows of one index of req no expert is named by more than 128 rows, a bound that some block reaches. `gate_weight`: index r holds expert r % 8. `up_weight`: index r holds expert r % 8. `down_weight`: index r holds expert r % 8.
All inputs are finite; a program needn't handle non-finite values.
Results may differ from a plain program's by a relative error of at most 0.007.
Values may be sent and summed in bfloat16 or wider, within the bound.
No kernel may reach another device: no remote copies, remote signals or barrier semaphores. Data moves between devices by JAX's collectives and lax.ppermute only.
A program may use at most 128 MiB of HBM per device.

v0:
```python
import jax
import jax.numpy as jnp
from jax import lax
from jax.sharding import PartitionSpec as P

E = 8
CAP = 128
epsilon = 1e-05


def shards(hidden, routes, route_weights, pre_gain, out_gain, gate_weight, up_weight, down_weight):
    row_count, col_part = hidden.shape
    tp_count = lax.axis_size("tp")
    req_count = lax.axis_size("req")
    full_width = col_part * tp_count
    copies = req_count // E
    slot_count = CAP // copies
    stream = hidden.astype(jnp.float32)
    whole_rows = lax.all_gather(hidden, "tp", axis=1, tiled=True).astype(jnp.float32)
    meansq = jnp.sum(whole_rows * whole_rows, axis=1) / full_width
    normed_in = (whole_rows * lax.rsqrt(meansq + epsilon)[:, None] * pre_gain[None, :]).astype(
        jnp.bfloat16
    )
    send_cols = normed_in.shape[1]
    top = routes.shape[1]
    chosen = routes.reshape(-1)
    onehot = (chosen[:, None] == jnp.arange(E, dtype=jnp.int32)[None, :]).astype(jnp.int32)
    slot_rank = jnp.sum((jnp.cumsum(onehot, axis=0) - 1) * onehot, axis=1)
    dest = slot_rank % copies * E + chosen
    out_idx = dest * slot_count + slot_rank // copies
    out_pairs = out_idx.reshape(row_count, top)
    slot_ids = jnp.arange(req_count * slot_count, dtype=jnp.int32)
    dispatch = jnp.zeros((req_count * slot_count, row_count), jnp.bool_)
    for k in range(top):
        dispatch = dispatch | (slot_ids[:, None] == out_pairs[None, :, k])
    outgoing = jnp.dot(
        dispatch.astype(jnp.bfloat16), normed_in, preferred_element_type=jnp.float32
    ).astype(jnp.bfloat16)
    outgoing = outgoing.reshape(req_count, slot_count, send_cols)
    pieces = lax.all_to_all(outgoing, "req", split_axis=0, concat_axis=0, tiled=True)
    sources, items, widths = pieces.shape
    flat_rows = pieces.reshape(sources * items, widths)
    gate_val = jnp.dot(flat_rows, gate_weight[0], preferred_element_type=jnp.float32)
    up_val = jnp.dot(flat_rows, up_weight[0], preferred_element_type=jnp.float32)
    activ = (jax.nn.silu(gate_val) * up_val).astype(jnp.bfloat16)
    partial_out = jnp.dot(activ, down_weight[0], preferred_element_type=jnp.float32)
    partial_out = lax.optimization_barrier(partial_out.astype(jnp.bfloat16)).astype(jnp.float32)
    summed = lax.psum_scatter(
        partial_out.reshape(sources, items, widths).astype(jnp.bfloat16),
        "tp",
        scatter_dimension=2,
        tiled=True,
    )
    returned = lax.all_to_all(summed, "req", split_axis=0, concat_axis=0, tiled=True)
    returned = returned.reshape(req_count * slot_count, col_part)
    picked = returned[out_idx].reshape(row_count, top, col_part).astype(jnp.float32)
    mixed = jnp.sum(picked * route_weights[:, :, None], axis=1)
    total_stream = stream + mixed
    out_sums = lax.psum(jnp.sum(total_stream * total_stream, axis=1), "tp")
    normed_out = (
        total_stream * lax.rsqrt(out_sums / full_width + epsilon)[:, None] * out_gain[None, :]
    )
    return (total_stream.astype(jnp.bfloat16), normed_out.astype(jnp.bfloat16))


def solution(mesh):
    return jax.shard_map(
        shards,
        mesh=mesh,
        in_specs=(
            P("req", "tp"),
            P("req", None),
            P("req", None),
            P(),
            P("tp"),
            P("req", None, "tp"),
            P("req", None, "tp"),
            P("req", "tp", None),
        ),
        out_specs=(P("req", "tp"), P("req", "tp")),
        check_vma=False,
    )
```

profile of v0, /device:TPU:0, one launch (start us, length us, event | category | flops | bytes accessed | tf_op | source)
XLA Modules:
  0.0 217.9 jit_solution(11316550749932052494)
XLA Ops:
  7.2 0.0 all-gather.2.cloned.1.call-start
  7.2 0.7 all-gather.2.cloned.1.call-update
  7.9 0.0 reduce-scatter.2.cloned.1.call-start
  7.9 0.8 copy.27
  8.8 0.1 eq.62
  8.9 0.1 eq.58
  9.1 1.1 reduce-window.6
  10.2 0.2 slice_reduce_fusion
  10.5 0.1 fusion.27
  10.6 0.1 reduce_sum.41
  10.7 0.1 copy.29
  10.8 0.7 fusion.31
  11.5 24.6 %all-gather.2.cloned.1.call-done = bf16[256,2048]{1,0:T(8,128)(2,1)} async-done(((bf16[256,512]{1,0:T(8,128)(2,1)}), bf16[256,2048]{1,0:T(8,128)(2,1)}) %all-gather.2.cloned.1.call-update) | async-done | bytes 1048592 | tf_op jit(solution)/shard_map/all_gather | solution.py:19
  36.1 0.0 slice-start
  36.1 1.7 fusion.16
  37.8 0.0 slice-start.1
  37.8 2.7 %convolution_convert_fusion = bf16[1024,2048]{1,0:T(8,128)(2,1)S(1)} fusion(bf16[256,2048]{1,0:T(8,128)(2,1)} %all-gather.2.cloned.1.call-done, f32[2048]{0:T(1024)} %param.11, f32[256]{0:T(256)S(1)} %add_rsqrt_fusion.1, s32[256]{0:T(256)S(1)} %bitcast.40, s32[256]{0:T(256)S(1)} %bitcast.39), kind=kOutput, calls=%fused_computation.8 | convolution fusion | flops 1078722560 | bytes 5254144 | tf_op jit(solution)/shard_map/dot_general | solution.py:36
  40.6 57.5 %all_to_all.10 = bf16[32,32,2048]{2,1,0:T(8,128)(2,1)S(1)} all-to-all(bf16[32,32,2048]{2,1,0:T(8,128)(2,1)S(1)} %bitcast.33), channel_id=1, replica_groups=mesh['req'=32,'tp'=4] {'req'}, dimensions={0} | all-to-all | bytes 8388608 | tf_op jit(solution)/shard_map/all_to_all | solution.py:40
  98.1 0.0 copy-start
  98.1 2.1 copy-done
  100.2 0.0 slice-done
  100.2 0.0 slice-done.1
  100.2 8.4 %fusion.4 = f32[1024,1408]{1,0:T(8,128)} fusion(bf16[1024,2048]{1,0:T(8,128)(2,1)S(1)} %bitcast.36, bf16[1,2048,1408]{2,1,0:T(8,128)(2,1)S(1)} %bitcast.43), kind=kOutput, calls=%fused_computation.5 | convolution fusion | flops 5905580032 | bytes 15728640 | tf_op jit(solution)/shard_map/dot_general | solution.py:43
  108.6 20.6 %fusion.10 = bf16[1024,2048]{1,0:T(8,128)(2,1)} fusion(bf16[1,1408,2048]{2,1,0:T(8,128)(2,1)} %param.15, f32[1024,1408]{1,0:T(8,128)} %fusion.4, bf16[1024,2048]{1,0:T(8,128)(2,1)} %bitcast.37, bf16[1,2048,1408]{2,1,0:T(8,128)(2,1)} %param.14), kind=kOutput, calls=%fused_computation.9 | convolution fusion | flops 11821907968 | bytes 25690112 | tf_op jit(solution)/shard_map/dot_general | solution.py:46
  129.3 0.0 copy-start.2
  129.3 0.0 reduce-scatter.2.cloned.1.call-update
  129.3 0.0 copy-start.1
  129.3 0.0 copy-start.3
  129.3 44.1 %reduce-scatter.2.cloned.1.call-done = bf16[32,32,512]{2,1,0:T(8,128)(2,1)} async-done(((bf16[32,32,2048]{2,1,0:T(8,128)(2,1)}), bf16[32,32,512]{2,1,0:T(8,128)(2,1)}) %reduce-scatter.2.cloned.1.call-update) | async-done | bytes 1048592 | tf_op jit(solution)/shard_map/reduce_scatter | solution.py:48
  173.4 7.4 %all-to-all-start.1 = ((bf16[32,32,512]{2,1,0:T(8,128)(2,1)}), bf16[32,32,512]{2,1,0:T(8,128)(2,1)S(1)}, u32[]{:S(2)}, u32[]{:S(2)}) async-start(bf16[32,32,512]{2,1,0:T(8,128)(2,1)} %reduce-scatter.2.cloned.1.call-done), calls=%async_computation.2 | async-start | bytes 2097152 | tf_op jit(solution)/shard_map/all_to_all | solution.py:54
  180.8 0.1 reshape.153
  181.0 0.0 copy-done.2
  181.0 0.1 copy.34
  181.2 16.3 %all-to-all-done.1 = bf16[32,32,512]{2,1,0:T(8,128)(2,1)S(1)} async-done(((bf16[32,32,512]{2,1,0:T(8,128)(2,1)}), bf16[32,32,512]{2,1,0:T(8,128)(2,1)S(1)}, u32[]{:S(2)}, u32[]{:S(2)}) %all-to-all-start.1) | async-done | bytes 1048608 | tf_op jit(solution)/shard_map/all_to_all | solution.py:54
  197.5 2.0 gather_fusion
  199.4 0.7 reshape.154
  200.1 1.3 multiply_reduce_fusion
  201.4 0.0 copy-done.1
  201.4 0.2 multiply_reduce_fusion.1
  201.6 8.6 %psum.7 = f32[256]{0:T(256)S(1)} all-reduce(f32[256]{0:T(256)S(1)} %multiply_reduce_fusion.1), channel_id=1, replica_groups=mesh['req'=32,'tp'=4] {'tp'}, use_global_device_ids=true, to_apply=%region_7.8 | all-reduce | flops 256 | bytes 2048 | tf_op jit(solution)/shard_map/psum | solution.py:59
  210.2 0.0 copy-done.3
  210.2 0.9 multiply_convert_fusion.1
  (9 shorter events, 0.1 us)
Async XLA Ops:
  7.2 29.0 %all-gather.2.cloned.1.call-start = ((), (), s32[]{:S(2)}) async-start(), calls=%async_computation.3 | async-start | bytes 1310720 | tf_op jit(solution)/shard_map/all_gather | solution.py:19
  7.9 165.5 %reduce-scatter.2.cloned.1.call-start = ((), (), s32[]{:S(2)}) async-start(), calls=%async_computation.4 | async-start | bytes 5242880 | tf_op jit(solution)/shard_map/reduce_scatter | solution.py:48
  36.1 64.1 %slice-start = ((s8[5767168]{0:T(1024)(128)(4,1)}), s8[4194304]{0:T(1024)(128)(4,1)S(1)}, s32[]{:S(2)}) async-start(s8[5767168]{0:T(1024)(128)(4,1)} %bitcast.42), calls=%async_computation.5 | async-start | bytes 8388608
  37.8 62.4 %slice-start.1 = ((s8[5767168]{0:T(1024)(128)(4,1)}), s8[1572864]{0:T(1024)(128)(4,1)S(1)}, s32[]{:S(2)}) async-start(s8[5767168]{0:T(1024)(128)(4,1)} %bitcast.42), calls=%async_computation.6 | async-start | bytes 3145728
  98.1 2.1 copy-start
  129.3 51.7 %copy-start.2 = (f32[256,2]{0,1:T(2,128)S(1)}, f32[256,2]{0,1:T(2,128)}, u32[]{:S(2)}) copy-start(f32[256,2]{0,1:T(2,128)} %param.10) | copy-start | bytes 6148
  129.3 72.1 %copy-start.1 = (bf16[256,512]{1,0:T(8,128)(2,1)S(1)}, bf16[256,512]{1,0:T(8,128)(2,1)}, u32[]{:S(2)}) copy-start(bf16[256,512]{1,0:T(8,128)(2,1)} %param.8) | copy-start | bytes 786436
  129.3 80.9 %copy-start.3 = (f32[512]{0:T(512)S(1)}, f32[512]{0:T(512)}, u32[]{:S(2)}) copy-start(f32[512]{0:T(512)} %param.12) | copy-start | bytes 6148
  173.4 24.1 %all-to-all-start.1 = ((bf16[32,32,512]{2,1,0:T(8,128)(2,1)}), bf16[32,32,512]{2,1,0:T(8,128)(2,1)S(1)}, u32[]{:S(2)}, u32[]{:S(2)}) async-start(bf16[32,32,512]{2,1,0:T(8,128)(2,1)} %reduce-scatter.2.cloned.1.call-done), calls=%async_computation.2 | async-start | bytes 2097152 | tf_op jit(solution)/shard_map/all_to_all | solution.py:54
Sparse Core Ops, SparseCore 0:
  9.7 26.4 all-gather.1
  129.4 43.9 reduce-scatter.1
where the time goes:
time: 218 us
  waiting for transfers between devices  85.7 us (39%)
  blocking collectives  66.1 us (30%)
  matrix products  31.8 us (15%)
  between operations  14.2 us (7%)
  starting transfers between devices  7.49 us (3%)
  local copies, waits for them, and re-layouts  6.53 us (3%)
  other arithmetic  6.04 us (3%)
    all_to_all x1, blocking collectives, shards(): lax.all_to_all(outgoing, 'req', split_axis=0, concat_axis=0, tiled=True)  57.5 us
    reduce_scatter x1, waiting for transfers between devices, shards(): lax.psum_scatter(partial_out.reshape(sources, items, widths).astype(jnp.b...  44.1 us
    all_gather x1, waiting for transfers between devices, shards(): lax.all_gather(hidden, 'tp', axis=1, tiled=True).astype(jnp.float32)  24.6 us
    dot_general x1, matrix products, shards(): jnp.dot(activ, down_weight[0], preferred_element_type=jnp.float32)  20.6 us
    all_to_all x1, waiting for transfers between devices, shards(): lax.all_to_all(summed, 'req', split_axis=0, concat_axis=0, tiled=True)  16.3 us
    psum x1, blocking collectives, shards(): out_sums = lax.psum(jnp.sum(total_stream * total_stream, axis=1), 'tp')  8.58 us
    dot_general x1, matrix products, shards(): jnp.dot(flat_rows, gate_weight[0], preferred_element_type=jnp.float32)  8.44 us
    all_to_all x1, starting transfers between devices, shards(): lax.all_to_all(summed, 'req', split_axis=0, concat_axis=0, tiled=True)  7.41 us
  transfers between devices with their start and end apart: 3, of which 3 were waited for; matrix products, arithmetic and copies ran while one was open for 2% of the time, Pallas kernels for 0%

commit v1 on v0

--- a/solution.py
+++ b/solution.py
@@ -16,7 +16,9 @@
     copies = req_count // E
     slot_count = CAP // copies
     stream = hidden.astype(jnp.float32)
-    whole_rows = lax.all_gather(hidden, "tp", axis=1, tiled=True).astype(jnp.float32)
+    whole_rows = jnp.concatenate(
+        lax.all_to_all(jnp.stack([hidden] * lax.axis_size("tp")), "tp", 0, 0), axis=1
+    ).astype(jnp.float32)
     meansq = jnp.sum(whole_rows * whole_rows, axis=1) / full_width
     normed_in = (whole_rows * lax.rsqrt(meansq + epsilon)[:, None] * pre_gain[None, :]).astype(
         jnp.bfloat16

time: 218 us -> 209 us (0.959)
  waiting for transfers between devices: 85.7 us -> 71 us
  starting transfers between devices: 7.49 us -> 12 us
    all_gather x1 -> x0, waiting for transfers between devices: 24.6 us -> none  [shards(): lax.all_gather(hidden, 'tp', axis=1, tiled=True).astype(jnp.float32)]
    all_to_all x0 -> x1, waiting for transfers between devices: none -> 11.5 us  [shards(): lax.all_to_all(jnp.stack([hidden] * lax.axis_size('tp')), 'tp', 0, 0)]
    all_to_all x0 -> x1, starting transfers between devices: none -> 4.55 us  [shards(): lax.all_to_all(jnp.stack([hidden] * lax.axis_size('tp')), 'tp', 0, 0)]
where the time goes in v1:
time: 209 us; the launch traced here: 208 us
  waiting for transfers between devices  71 us (34%)
  blocking collectives  67.2 us (32%)
  matrix products  30.4 us (15%)
  between operations  14.2 us (7%)
  starting transfers between devices  12 us (6%)
  local copies, waits for them, and re-layouts  8.68 us (4%)
  other arithmetic  5.03 us (2%)
    all_to_all x1, blocking collectives, shards(): lax.all_to_all(outgoing, 'req', split_axis=0, concat_axis=0, tiled=True)  58.6 us
    reduce_scatter x1, waiting for transfers between devices, shards(): lax.psum_scatter(partial_out.reshape(sources, items, widths).astype(jnp.b...  43.2 us
    dot_general x1, matrix products, shards(): jnp.dot(activ, down_weight[0], preferred_element_type=jnp.float32)  20.6 us
    all_to_all x1, waiting for transfers between devices, shards(): lax.all_to_all(summed, 'req', split_axis=0, concat_axis=0, tiled=True)  16.3 us
    all_to_all x1, waiting for transfers between devices, shards(): lax.all_to_all(jnp.stack([hidden] * lax.axis_size('tp')), 'tp', 0, 0)  11.5 us
    psum x1, blocking collectives, shards(): out_sums = lax.psum(jnp.sum(total_stream * total_stream, axis=1), 'tp')  8.6 us
    dot_general x1, matrix products, shards(): jnp.dot(flat_rows, gate_weight[0], preferred_element_type=jnp.float32)  8.44 us
    all_to_all x1, starting transfers between devices, shards(): lax.all_to_all(summed, 'req', split_axis=0, concat_axis=0, tiled=True)  7.41 us
  transfers between devices with their start and end apart: 3, of which 3 were waited for; matrix products, arithmetic and copies ran while one was open for 2% of the time, Pallas kernels for 0%

profile of v1, /device:TPU:0, one launch (start us, length us, event | category | flops | bytes accessed | tf_op | source)
XLA Modules:
  0.0 208.5 jit_solution(7438943868932061509)
XLA Ops:
  7.2 0.0 copy-start.2
  7.2 1.1 copy.35
  8.3 1.1 stack.2
  9.3 4.5 %all-to-all-start = ((bf16[4,256,512]{1,2,0:T(8,128)(2,1)}), bf16[4,256,512]{1,2,0:T(8,128)(2,1)S(1)}, u32[]{:S(2)}, u32[]{:S(2)}) async-start(bf16[4,256,512]{1,2,0:T(8,128)(2,1)} %stack.2), calls=%async_computation | async-start | bytes 2097152 | tf_op jit(solution)/shard_map/all_to_all | solution.py:20
  13.9 0.0 reduce-scatter.2.cloned.1.call-start
  13.9 0.8 copy.29
  14.7 0.1 eq.62
  14.8 0.1 eq.58
  15.0 1.1 reduce-window.6
  16.1 0.2 slice_reduce_fusion
  16.4 0.1 fusion.23
  16.5 0.1 reduce_sum.41
  16.6 0.1 copy.31
  16.7 0.7 fusion.27
  17.4 11.5 %all-to-all-done = bf16[4,256,512]{1,2,0:T(8,128)(2,1)S(1)} async-done(((bf16[4,256,512]{1,2,0:T(8,128)(2,1)}), bf16[4,256,512]{1,2,0:T(8,128)(2,1)S(1)}, u32[]{:S(2)}, u32[]{:S(2)}) %all-to-all-start) | async-done | bytes 1048608 | tf_op jit(solution)/shard_map/all_to_all | solution.py:20
  29.0 0.3 multiply_reduce_fusion
  29.3 0.0 copy-done.2
  29.3 0.0 slice-start
  29.3 0.3 fusion.17
  29.6 0.0 slice-start.1
  29.7 1.3 convolution_convert_fusion
  31.0 58.6 %all_to_all.15 = bf16[32,32,2048]{2,1,0:T(8,128)(2,1)S(1)} all-to-all(bf16[32,32,2048]{2,1,0:T(8,128)(2,1)S(1)} %bitcast.42), channel_id=1, replica_groups=mesh['req'=32,'tp'=4] {'req'}, dimensions={0} | all-to-all | bytes 8388608 | tf_op jit(solution)/shard_map/all_to_all | solution.py:42
  89.6 0.0 copy-start
  89.6 2.1 copy-done
  91.6 0.0 slice-done
  91.6 0.0 slice-done.1
  91.7 8.4 %fusion.4 = f32[1024,1408]{1,0:T(8,128)} fusion(bf16[1024,2048]{1,0:T(8,128)(2,1)S(1)} %bitcast.45, bf16[1,2048,1408]{2,1,0:T(8,128)(2,1)S(1)} %bitcast.52), kind=kOutput, calls=%fused_computation.5 | convolution fusion | flops 5905580032 | bytes 15728640 | tf_op jit(solution)/shard_map/dot_general | solution.py:45
  100.1 20.6 %fusion.10 = bf16[1024,2048]{1,0:T(8,128)(2,1)} fusion(bf16[1,1408,2048]{2,1,0:T(8,128)(2,1)} %param.15, f32[1024,1408]{1,0:T(8,128)} %fusion.4, bf16[1024,2048]{1,0:T(8,128)(2,1)} %bitcast.46, bf16[1,2048,1408]{2,1,0:T(8,128)(2,1)} %param.14), kind=kOutput, calls=%fused_computation.9 | convolution fusion | flops 11821907968 | bytes 25690112 | tf_op jit(solution)/shard_map/dot_general | solution.py:48
  120.7 0.0 copy-start.3
  120.7 0.0 reduce-scatter.2.cloned.1.call-update
  120.8 0.0 copy-start.1
  120.8 0.0 copy-start.4
  120.8 43.2 %reduce-scatter.2.cloned.1.call-done = bf16[32,32,512]{2,1,0:T(8,128)(2,1)} async-done(((bf16[32,32,2048]{2,1,0:T(8,128)(2,1)}), bf16[32,32,512]{2,1,0:T(8,128)(2,1)}) %reduce-scatter.2.cloned.1.call-update) | async-done | bytes 1048592 | tf_op jit(solution)/shard_map/reduce_scatter | solution.py:50
  164.0 7.4 %all-to-all-start.2 = ((bf16[32,32,512]{2,1,0:T(8,128)(2,1)}), bf16[32,32,512]{2,1,0:T(8,128)(2,1)S(1)}, u32[]{:S(2)}, u32[]{:S(2)}) async-start(bf16[32,32,512]{2,1,0:T(8,128)(2,1)} %reduce-scatter.2.cloned.1.call-done), calls=%async_computation.3 | async-start | bytes 2097152 | tf_op jit(solution)/shard_map/all_to_all | solution.py:56
  171.4 0.1 reshape.159
  171.5 0.0 copy-done.3
  171.5 0.1 copy.37
  171.7 16.3 %all-to-all-done.2 = bf16[32,32,512]{2,1,0:T(8,128)(2,1)S(1)} async-done(((bf16[32,32,512]{2,1,0:T(8,128)(2,1)}), bf16[32,32,512]{2,1,0:T(8,128)(2,1)S(1)}, u32[]{:S(2)}, u32[]{:S(2)}) %all-to-all-start.2) | async-done | bytes 1048608 | tf_op jit(solution)/shard_map/all_to_all | solution.py:56
  188.0 2.0 gather_fusion
  190.0 0.7 reshape.161
  190.7 1.3 multiply_reduce_fusion.1
  192.0 0.0 copy-done.1
  192.0 0.2 multiply_reduce_fusion.2
  192.2 8.6 %psum.7 = f32[256]{0:T(256)S(1)} all-reduce(f32[256]{0:T(256)S(1)} %multiply_reduce_fusion.2), channel_id=1, replica_groups=mesh['req'=32,'tp'=4] {'tp'}, use_global_device_ids=true, to_apply=%region_7.8 | all-reduce | flops 256 | bytes 2048 | tf_op jit(solution)/shard_map/psum | solution.py:61
  200.8 0.0 copy-done.4
  200.8 0.9 multiply_convert_fusion.1
  (9 shorter events, 0.1 us)
Async XLA Ops:
  7.2 22.1 %copy-start.2 = (f32[2048]{0:T(1024)S(1)}, f32[2048]{0:T(1024)}, u32[]{:S(2)}) copy-start(f32[2048]{0:T(1024)} %param.11) | copy-start | bytes 24580
  9.3 19.6 %all-to-all-start = ((bf16[4,256,512]{1,2,0:T(8,128)(2,1)}), bf16[4,256,512]{1,2,0:T(8,128)(2,1)S(1)}, u32[]{:S(2)}, u32[]{:S(2)}) async-start(bf16[4,256,512]{1,2,0:T(8,128)(2,1)} %stack.2), calls=%async_computation | async-start | bytes 2097152 | tf_op jit(solution)/shard_map/all_to_all | solution.py:20
  13.9 150.1 %reduce-scatter.2.cloned.1.call-start = ((), (), s32[]{:S(2)}) async-start(), calls=%async_computation.4 | async-start | bytes 5242880 | tf_op jit(solution)/shard_map/reduce_scatter | solution.py:50
  29.3 62.4 %slice-start = ((s8[5767168]{0:T(1024)(128)(4,1)}), s8[4194304]{0:T(1024)(128)(4,1)S(1)}, s32[]{:S(2)}) async-start(s8[5767168]{0:T(1024)(128)(4,1)} %bitcast.51), calls=%async_computation.5 | async-start | bytes 8388608
  29.6 62.0 %slice-start.1 = ((s8[5767168]{0:T(1024)(128)(4,1)}), s8[1572864]{0:T(1024)(128)(4,1)S(1)}, s32[]{:S(2)}) async-start(s8[5767168]{0:T(1024)(128)(4,1)} %bitcast.51), calls=%async_computation.6 | async-start | bytes 3145728
  89.6 2.1 copy-start
  120.7 50.8 %copy-start.3 = (f32[256,2]{0,1:T(2,128)S(1)}, f32[256,2]{0,1:T(2,128)}, u32[]{:S(2)}) copy-start(f32[256,2]{0,1:T(2,128)} %param.10) | copy-start | bytes 6148
  120.8 71.2 %copy-start.1 = (bf16[256,512]{1,0:T(8,128)(2,1)S(1)}, bf16[256,512]{1,0:T(8,128)(2,1)}, u32[]{:S(2)}) copy-start(bf16[256,512]{1,0:T(8,128)(2,1)} %param.8) | copy-start | bytes 786436
  120.8 80.0 %copy-start.4 = (f32[512]{0:T(512)S(1)}, f32[512]{0:T(512)}, u32[]{:S(2)}) copy-start(f32[512]{0:T(512)} %param.12) | copy-start | bytes 6148
  164.0 24.1 %all-to-all-start.2 = ((bf16[32,32,512]{2,1,0:T(8,128)(2,1)}), bf16[32,32,512]{2,1,0:T(8,128)(2,1)S(1)}, u32[]{:S(2)}, u32[]{:S(2)}) async-start(bf16[32,32,512]{2,1,0:T(8,128)(2,1)} %reduce-scatter.2.cloned.1.call-done), calls=%async_computation.3 | async-start | bytes 2097152 | tf_op jit(solution)/shard_map/all_to_all | solution.py:56
Sparse Core Ops, SparseCore 0:
  120.9 43.0 reduce-scatter.1
